TPU v7x, 32 devices: a whole 2x2x4 slice. The times are simulated.
32 devices in a mesh: dp: 2 (over x), mp: 16 (over z, y, core).
Axes of the slice: x: 2, y: 2, z: 4, core: 2. Of those that a mesh axis runs over, the one named last changes fastest.
Arguments:
- node_features: bfloat16 [512, 6144], P('mp', 'dp'), may hold values from -6 to 6
- weights_one: bfloat16 [1024, 512], replicated, may hold values from -0.25 to 0.25
- weights_two: bfloat16 [1024, 512], replicated, may hold values from -0.25 to 0.25
- neighbor_owner: int32 [6144, 8], P('dp'), may hold values from 0 to 15, all different within a row; in each aligned block of 192 rows (0 to 191, 192 to 383, ...) at most 144 rows name the same one
- neighbor_row: int32 [6144, 8], P('dp'), may hold values from 0 to 191
- neighbor_count: int32 [6144], P('dp'), may hold values from 4 to 8
- cotangent: bfloat16 [6144, 512], P(('dp', 'mp')), may hold values from -0.076171875 to 0.076171875
Outputs:
- node_output: bfloat16 [6144, 512], P(('dp', 'mp'))
- weight_grads: float32 [2048, 512], P(('dp', 'mp'))
Inputs may be any that keep to these rules, and one draw needn't show every extreme that they name: `neighbor_owner`: each row names 8 different owners; among the rows of one device (aligned blocks of 192 rows) no owner is named more than 144 times, and in some block one owner exactly 144 times. Slots k >= neighbor_count[r] are padding and carry no edge.
All inputs are finite; a program needn't handle non-finite values.
Results may differ from a plain program's by a relative error of at most 0.0052.
Values may be sent and summed in bfloat16 or wider, within the bound.
No kernel may reach another device: no remote copies, remote signals or barrier semaphores. Data moves between devices by JAX's collectives and lax.ppermute only.
A program may use at most 64 MiB of HBM per device.

v0:
```python
import jax
import jax.numpy as jnp
from jax import lax
from jax.sharding import PartitionSpec as P


def column_mean(table, indices, live, inverse):
    total = jnp.zeros((table.shape[0], indices.shape[1]), jnp.float32)
    for slot_index in range(indices.shape[0]):
        picked = jnp.take(table, indices[slot_index], axis=1)
        kept = jnp.where(live[slot_index][None, :], picked, jnp.zeros_like(picked))
        total = total + kept.astype(jnp.float32)
    return (total * inverse[None, :]).astype(jnp.bfloat16)


def silu_slope(values):
    sigmoid = jax.nn.sigmoid(values)
    return sigmoid * (1.0 + values * (1.0 - sigmoid))


def contract(left, right, left_dim, right_dim):
    return lax.dot_general(
        left, right, (((left_dim,), (right_dim,)), ((), ())), preferred_element_type=jnp.float32
    )


def shards(
    node_features, weights_one, weights_two, neighbor_owner, neighbor_row, neighbor_count, cotangent
):
    devices = lax.axis_size("mp")
    own_index = lax.axis_index("mp")
    node_dev = cotangent.shape[0]
    all_nodes = neighbor_owner.shape[0]
    fanout = neighbor_owner.shape[1]
    feat_width = weights_one.shape[0] // 2
    hidden = weights_one.shape[1]
    capacity = 3 * node_dev * fanout // (2 * devices)
    live = lax.broadcasted_iota(jnp.int32, (all_nodes, fanout), 1) < neighbor_count[:, None]
    inverse_all = 1.0 / neighbor_count.astype(jnp.float32)
    owner_ids = lax.broadcasted_iota(jnp.int32, (devices, 1, 1), 0)
    match = (neighbor_owner[None, :, :] == owner_ids) & live[None, :, :]
    rowsel = jnp.max(jnp.where(match, neighbor_row[None, :, :], -1), axis=2)
    has = rowsel >= 0
    with jax.named_scope("layer_one_mean"):
        if all_nodes * all_nodes <= 4096 * 4096:
            row_ids = lax.broadcasted_iota(jnp.int32, (1, node_dev, 1), 1)
            adjacency = (rowsel[:, None, :] == row_ids).astype(jnp.bfloat16)
            adjacency = adjacency.reshape(devices * node_dev, all_nodes)
            summed = contract(node_features, adjacency, 1, 0)
            agg_one_cols = (summed * inverse_all[None, :]).astype(jnp.bfloat16)
        else:
            owner_slots = neighbor_owner.T
            global_ids = owner_slots * node_dev + neighbor_row.T
            agg_one_cols = column_mean(node_features, global_ids, live.T, inverse_all)
    own_feats, own_agg_one = (
        lax.all_to_all(node_features, "mp", split_axis=1, concat_axis=0, tiled=True),
        lax.all_to_all(agg_one_cols, "mp", split_axis=1, concat_axis=0, tiled=True),
    )
    pre_one = contract(weights_one[:feat_width], own_feats, 0, 0) + contract(
        weights_one[feat_width:], own_agg_one, 0, 0
    )
    hidden_one = jax.nn.silu(pre_one).astype(jnp.bfloat16)
    with jax.named_scope("slot_tables"):
        blocks = has.reshape(devices * devices, node_dev).astype(jnp.bfloat16)
        before = (
            lax.broadcasted_iota(jnp.int32, (node_dev, node_dev), 0)
            < lax.broadcasted_iota(jnp.int32, (node_dev, node_dev), 1)
        ).astype(jnp.bfloat16)
        ranks = contract(blocks, before, 1, 0).astype(jnp.int32).reshape(devices, devices, node_dev)
        has_blocks = has.reshape(devices, devices, node_dev)
        rows_blocks = rowsel.reshape(devices, devices, node_dev)
        cap_ids = lax.broadcasted_iota(jnp.int32, (1, capacity, 1), 1)
        own_rank = lax.dynamic_index_in_dim(ranks, own_index, 1, keepdims=False)
        own_has = lax.dynamic_index_in_dim(has_blocks, own_index, 1, keepdims=False)
        gathered = ((own_rank[:, None, :] == cap_ids) & own_has[:, None, :]).astype(jnp.bfloat16)
        gathered = gathered.reshape(devices * capacity, node_dev)
        req_rank = lax.dynamic_index_in_dim(ranks, own_index, 0, keepdims=False)
        req_has = lax.dynamic_index_in_dim(has_blocks, own_index, 0, keepdims=False)
        req_rows = lax.dynamic_index_in_dim(rows_blocks, own_index, 0, keepdims=False)
        pick = ((req_rank[:, None, :] == cap_ids) & req_has[:, None, :]).astype(jnp.bfloat16)
        row_ids = lax.broadcasted_iota(jnp.int32, (1, 1, node_dev), 2)
        which = (req_rows[:, :, None] == row_ids).astype(jnp.bfloat16)
        asked = lax.dot_general(
            pick, which, (((2,), (1,)), ((0,), (0,))), preferred_element_type=jnp.float32
        )
        asked = asked.astype(jnp.bfloat16).reshape(devices * capacity, node_dev)
    own_inverse = lax.dynamic_slice_in_dim(inverse_all, own_index * node_dev, node_dev, 0)
    outgoing = contract(hidden_one, asked, 1, 1).astype(jnp.bfloat16)
    incoming = lax.all_to_all(outgoing, "mp", split_axis=1, concat_axis=1, tiled=True)
    total = contract(incoming, gathered, 1, 0)
    agg_two = (total * own_inverse[None, :]).astype(jnp.bfloat16)
    self_two = weights_two[:hidden]
    neigh_two = weights_two[hidden:]
    node_output = (
        contract(hidden_one, self_two, 0, 0) + contract(agg_two, neigh_two, 0, 0)
    ).astype(jnp.bfloat16)
    down_self = contract(self_two, cotangent, 1, 1)
    down_neigh = (contract(neigh_two, cotangent, 1, 1) * own_inverse[None, :]).astype(jnp.bfloat16)
    outgoing_grad = contract(down_neigh, gathered, 1, 1).astype(jnp.bfloat16)
    incoming_grad = lax.all_to_all(outgoing_grad, "mp", split_axis=1, concat_axis=1, tiled=True)
    neighbor_sum = contract(incoming_grad, asked, 1, 0)
    grad_hidden = down_self + neighbor_sum
    grad_pre = (grad_hidden * silu_slope(pre_one)).astype(jnp.bfloat16)
    terms = jnp.concatenate(
        [
            contract(own_feats, grad_pre, 1, 1),
            contract(own_agg_one, grad_pre, 1, 1),
            contract(hidden_one, cotangent, 1, 0),
            contract(agg_two, cotangent, 1, 0),
        ],
        axis=0,
    )
    weight_grads = lax.psum_scatter(terms, ("dp", "mp"), scatter_dimension=0, tiled=True)
    return (node_output, weight_grads)


def solution(mesh):
    in_specs = (
        P("mp", "dp"),
        P(),
        P(),
        P("dp", None),
        P("dp", None),
        P("dp"),
        P(("dp", "mp"), None),
    )
    out_specs = (P(("dp", "mp"), None), P(("dp", "mp"), None))
    return jax.shard_map(shards, mesh=mesh, in_specs=in_specs, out_specs=out_specs, check_vma=False)
```

profile of v0, /device:TPU:0, one launch (start us, length us, event | category | flops | bytes accessed | tf_op | source)
XLA Modules:
  0.0 325.1 jit_solution(16609977738096543799)
XLA Ops:
  7.2 1.3 all_to_all.40
  8.5 0.8 copy.27
  9.3 7.4 %all-to-all-start = ((bf16[32,16,192]{2,0,1:T(8,128)(2,1)}), bf16[32,16,192]{2,0,1:T(8,128)(2,1)S(1)}, u32[]{:S(2)}, u32[]{:S(2)}) async-start(bf16[32,16,192]{2,0,1:T(8,128)(2,1)} %copy.27), calls=%async_computation | async-start | bytes 524288 | tf_op jit(solution)/shard_map/all_to_all | solution.py:56
  16.7 0.7 iota_compare_fusion.9
  17.4 0.7 convert_divide_fusion
  18.2 1.8 select_reduce_fusion
  20.0 9.7 %bitcast_compare_fusion = pred[3072,3072]{1,0:T(32,128)(4,1)} fusion(s32[3072]{0:T(1024)S(1)} %eq.95, s32[16,3072]{1,0:T(8,128)S(1)} %select_reduce_fusion), kind=kLoop, calls=%fused_computation | loop fusion | flops 9437184 | bytes 9646080 | tf_op jit(solution)/shard_map/layer_one_mean/eq | solution.py:47
  29.9 8.5 %fusion.1 = bf16[32,3072]{1,0:T(8,128)(2,1)S(1)} fusion(pred[3072,3072]{1,0:T(32,128)(4,1)} %bitcast_compare_fusion, bf16[32,3072]{1,0:T(8,128)(2,1)S(1)} %copy-done.7, f32[3072]{0:T(1024)S(1)} %convert_divide_fusion), kind=kOutput, calls=%fused_computation.6 | convolution fusion | flops 604176384 | bytes 9842688 | tf_op jit(solution)/shard_map/layer_one_mean/dot_general | solution.py:22
  38.4 0.4 convolution_convert_fusion.2
  39.3 0.8 copy.28
  40.4 6.1 %all-to-all-start.1 = ((bf16[32,16,192]{2,0,1:T(8,128)(2,1)}), bf16[32,16,192]{2,0,1:T(8,128)(2,1)}, u32[]{:S(2)}, u32[]{:S(2)}) async-start(bf16[32,16,192]{2,0,1:T(8,128)(2,1)} %copy.28), calls=%async_computation.1 | async-start | bytes 524288 | tf_op jit(solution)/shard_map/all_to_all | solution.py:57
  46.7 0.5 fusion.8
  47.2 2.2 convolution_convert_fusion
  49.4 2.5 copy.31
  51.9 4.6 %all-to-all-done.1 = bf16[32,16,192]{2,0,1:T(8,128)(2,1)} async-done(((bf16[32,16,192]{2,0,1:T(8,128)(2,1)}), bf16[32,16,192]{2,0,1:T(8,128)(2,1)}, u32[]{:S(2)}, u32[]{:S(2)}) %all-to-all-start.1) | async-done | bytes 196640 | tf_op jit(solution)/shard_map/all_to_all | solution.py:57
  56.5 3.7 %all-to-all-start.3 = ((bf16[512,16,144]{0,2,1:T(8,128)(2,1)}), bf16[512,16,144]{0,2,1:T(8,128)(2,1)S(1)}, u32[]{:S(2)}, u32[]{:S(2)}) async-start(bf16[512,16,144]{0,2,1:T(8,128)(2,1)} %bitcast.16), calls=%async_computation.3 | async-start | bytes 4718592 | tf_op jit(solution)/shard_map/all_to_all | solution.py:100
  60.3 0.8 dynamic-slice_bitcast_fusion
  61.1 1.3 fusion.11
  62.8 1.3 fusion.18
  64.1 2.4 convolution_convert_fusion.1
  66.5 4.3 %copy.30 = bf16[512,2304]{0,1:T(8,128)(2,1)} copy(bf16[512,2304]{1,0:T(8,128)(2,1)} %convolution_convert_fusion.1) | data formatting | bytes 4718592 | tf_op jit(solution)/shard_map/convert_element_type | solution.py:88
  70.8 35.1 %all-to-all-done.3 = bf16[512,16,144]{0,2,1:T(8,128)(2,1)S(1)} async-done(((bf16[512,16,144]{0,2,1:T(8,128)(2,1)}), bf16[512,16,144]{0,2,1:T(8,128)(2,1)S(1)}, u32[]{:S(2)}, u32[]{:S(2)}) %all-to-all-start.3) | async-done | bytes 2359328 | tf_op jit(solution)/shard_map/all_to_all | solution.py:100
  105.9 12.3 %all-to-all-start.2 = ((bf16[512,16,144]{0,2,1:T(8,128)(2,1)}), bf16[512,16,144]{0,2,1:T(8,128)(2,1)}, u32[]{:S(2)}, u32[]{:S(2)}) async-start(bf16[512,16,144]{0,2,1:T(8,128)(2,1)} %bitcast.12), calls=%async_computation.2 | async-start | bytes 4718592 | tf_op jit(solution)/shard_map/all_to_all | solution.py:89
  118.2 1.4 fusion.42
  119.6 2.0 convolution_bitcast_fusion.1
  122.0 1.2 fusion.43
  123.5 40.4 %all-to-all-done.2 = bf16[512,16,144]{0,2,1:T(8,128)(2,1)} async-done(((bf16[512,16,144]{0,2,1:T(8,128)(2,1)}), bf16[512,16,144]{0,2,1:T(8,128)(2,1)}, u32[]{:S(2)}, u32[]{:S(2)}) %all-to-all-start.2) | async-done | bytes 2359328 | tf_op jit(solution)/shard_map/all_to_all | solution.py:89
  163.9 2.6 fusion.26
  166.9 2.4 pad_maximum_fusion
  169.3 1.2 copy-done.4
  170.8 1.0 fusion.30
  171.7 146.5 %reduce-scatter.2.cloned.1.call-done = f32[64,512]{1,0:T(8,128)} async-done(((f32[2048,512]{1,0:T(8,128)}), f32[64,512]{1,0:T(8,128)}) %reduce-scatter.2.cloned.1.call-update) | async-done | bytes 131088 | tf_op jit(solution)/shard_map/reduce_scatter | solution.py:113
  (41 shorter events, 2.8 us)
Async XLA Ops:
  7.2 40.0 %copy-start = (bf16[192,512]{1,0:T(8,128)(2,1)S(1)}, bf16[192,512]{1,0:T(8,128)(2,1)}, u32[]{:S(2)}) copy-start(bf16[192,512]{1,0:T(8,128)(2,1)} %param.13) | copy-start | bytes 589828
  9.3 31.1 %all-to-all-start = ((bf16[32,16,192]{2,0,1:T(8,128)(2,1)}), bf16[32,16,192]{2,0,1:T(8,128)(2,1)S(1)}, u32[]{:S(2)}, u32[]{:S(2)}) async-start(bf16[32,16,192]{2,0,1:T(8,128)(2,1)} %copy.27), calls=%async_computation | async-start | bytes 524288 | tf_op jit(solution)/shard_map/all_to_all | solution.py:56
  20.0 9.9 %copy-start.7 = (bf16[32,3072]{1,0:T(8,128)(2,1)S(1)}, bf16[32,3072]{1,0:T(8,128)(2,1)}, u32[]{:S(2)}) copy-start(bf16[32,3072]{1,0:T(8,128)(2,1)} %param.7) | copy-start | bytes 589828
  39.0 7.7 %copy-start.1 = (s32[16,16,192]{2,1,0:T(8,128)}, s32[16,16,192]{2,1,0:T(8,128)S(1)}, u32[]{:S(2)}) copy-start(s32[16,16,192]{2,1,0:T(8,128)S(1)} %reduce_max.12) | copy-start | bytes 589828
  40.2 6.4 %copy-start.6 = (s32[256,192]{1,0:T(8,128)}, s32[256,192]{1,0:T(8,128)S(1)}, u32[]{:S(2)}) copy-start(s32[256,192]{1,0:T(8,128)S(1)} %copy.29) | copy-start | bytes 589828
  40.4 16.2 %all-to-all-start.1 = ((bf16[32,16,192]{2,0,1:T(8,128)(2,1)}), bf16[32,16,192]{2,0,1:T(8,128)(2,1)}, u32[]{:S(2)}, u32[]{:S(2)}) async-start(bf16[32,16,192]{2,0,1:T(8,128)(2,1)} %copy.28), calls=%async_computation.1 | async-start | bytes 524288 | tf_op jit(solution)/shard_map/all_to_all | solution.py:57
  56.5 49.3 %all-to-all-start.3 = ((bf16[512,16,144]{0,2,1:T(8,128)(2,1)}), bf16[512,16,144]{0,2,1:T(8,128)(2,1)S(1)}, u32[]{:S(2)}, u32[]{:S(2)}) async-start(bf16[512,16,144]{0,2,1:T(8,128)(2,1)} %bitcast.16), calls=%async_computation.3 | async-start | bytes 4718592 | tf_op jit(solution)/shard_map/all_to_all | solution.py:100
  60.3 2.2 copy-start.2
  62.5 1.7 copy-start.8
  105.9 58.0 %all-to-all-start.2 = ((bf16[512,16,144]{0,2,1:T(8,128)(2,1)}), bf16[512,16,144]{0,2,1:T(8,128)(2,1)}, u32[]{:S(2)}, u32[]{:S(2)}) async-start(bf16[512,16,144]{0,2,1:T(8,128)(2,1)} %bitcast.12), calls=%async_computation.2 | async-start | bytes 4718592 | tf_op jit(solution)/shard_map/all_to_all | solution.py:89
  118.2 200.1 %reduce-scatter.2.cloned.1.call-start = ((), (), s32[]{:S(2)}) async-start(), calls=%async_computation.5 | async-start | bytes 4325376 | tf_op jit(solution)/shard_map/reduce_scatter | solution.py:113
  119.6 2.0 copy-start.3
  163.9 3.0 copy-start.5
  169.3 1.2 copy-start.4
Sparse Core Ops, SparseCore 0:
  169.4 148.7 reduce-scatter.1
where the time goes:
time: 326 us; the launch traced here: 325 us
  waiting for transfers between devices  227 us (70%)
  starting transfers between devices  29.5 us (9%)
  matrix products  25.9 us (8%)
  other arithmetic  15.9 us (5%)
  between operations  14.4 us (4%)
  local copies, waits for them, and re-layouts  12.7 us (4%)
    reduce_scatter x1, waiting for transfers between devices, shards(): lax.psum_scatter(terms, ('dp', 'mp'), scatter_dimension=0, tiled=True)  147 us
    all_to_all x1, waiting for transfers between devices, shards(): lax.all_to_all(outgoing, 'mp', split_axis=1, concat_axis=1, tiled=True)  40.4 us
    all_to_all x1, waiting for transfers between devices, shards(): lax.all_to_all(outgoing_grad, 'mp', split_axis=1, concat_axis=1, tiled=True)  35.1 us
    dot_general x15, matrix products, contract(): lax.dot_general(left, right, (((left_dim,), (right_dim,)), ((), ())), pre...  24.6 us
    all_to_all x1, starting transfers between devices, shards(): lax.all_to_all(outgoing, 'mp', split_axis=1, concat_axis=1, tiled=True)  12.3 us
    eq x1, other arithmetic, shards(): adjacency = (rowsel[:, None, :] == row_ids).astype(jnp.bfloat16)  9.7 us
    all_to_all x1, starting transfers between devices, shards(): lax.all_to_all(node_features, 'mp', split_axis=1, concat_axis=0, tiled=True)  7.39 us
  transfers between devices with their start and end apart: 5, of which 4 were waited for; matrix products, arithmetic and copies ran while one was open for 14% of the time, Pallas kernels for 0%

commit v1 on v0

--- a/solution.py
+++ b/solution.py
@@ -2,6 +2,30 @@
 import jax.numpy as jnp
 from jax import lax
 from jax.sharding import PartitionSpec as P
+
+
+def in_blocks(x, dim, size):
+    lengths = x.shape
+    pieces = x.reshape(*lengths[:dim], size, lengths[dim] // size, *lengths[dim + 1 :])
+    return jnp.moveaxis(pieces, dim, 0)
+
+
+def joined_along(blocks, dim):
+    blocks = jnp.moveaxis(blocks, 0, dim)
+    lengths = blocks.shape
+    return blocks.reshape(*lengths[:dim], lengths[dim] * lengths[dim + 1], *lengths[dim + 2 :])
+
+
+def rotated_exchange(x, axis, split_dim, concat_dim):
+    size, index = (lax.axis_size(axis), lax.axis_index(axis))
+    blocks = in_blocks(x, split_dim, size)
+    whole = blocks
+    for step in range(1, size):
+        target, source = ((index + step) % size, (index - step) % size)
+        sent = lax.dynamic_index_in_dim(blocks, target, 0)
+        other = lax.ppermute(sent, axis, [(i, (i + step) % size) for i in range(size)])
+        whole = lax.dynamic_update_slice_in_dim(whole, other, source, axis=0)
+    return joined_along(whole, concat_dim)
 
 
 def column_mean(table, indices, live, inverse):
@@ -86,7 +110,7 @@
         asked = asked.astype(jnp.bfloat16).reshape(devices * capacity, node_dev)
     own_inverse = lax.dynamic_slice_in_dim(inverse_all, own_index * node_dev, node_dev, 0)
     outgoing = contract(hidden_one, asked, 1, 1).astype(jnp.bfloat16)
-    incoming = lax.all_to_all(outgoing, "mp", split_axis=1, concat_axis=1, tiled=True)
+    incoming = rotated_exchange(outgoing, "mp", 1, 1)
     total = contract(incoming, gathered, 1, 0)
     agg_two = (total * own_inverse[None, :]).astype(jnp.bfloat16)
     self_two = weights_two[:hidden]

time: 326 us -> 327 us (level)
  starting transfers between devices: 29.5 us -> 62.4 us
  waiting for transfers between devices: 227 us -> 198 us
    ppermute x0 -> x15, waiting for transfers between devices: none -> 51.3 us  [rotated_exchange(): lax.ppermute(sent, axis, [(i, (i + step) % size) for i in range(size)])]
    ppermute x0 -> x15, starting transfers between devices: none -> 44.5 us  [rotated_exchange(): lax.ppermute(sent, axis, [(i, (i + step) % size) for i in range(size)])]
    all_to_all x1 -> x0, waiting for transfers between devices: 40.4 us -> none  [shards(): lax.all_to_all(outgoing, 'mp', split_axis=1, concat_axis=1, tiled=True)]
    all_to_all x1, waiting for transfers between devices: 35.1 us -> 0.01 us  [shards(): lax.all_to_all(outgoing_grad, 'mp', split_axis=1, concat_axis=1, tiled=True)]
    all_to_all x1 -> x0, starting transfers between devices: 12.3 us -> none  [shards(): lax.all_to_all(outgoing, 'mp', split_axis=1, concat_axis=1, tiled=True)]
    reduce_scatter x1, waiting for transfers between devices: 147 us -> 142 us  [shards(): lax.psum_scatter(terms, ('dp', 'mp'), scatter_dimension=0, tiled=True)]
  transfers between devices with their start and end apart: 5 -> 19, of which waited for: 4 -> 8; matrix products, arithmetic and copies ran while one was open for 14% -> 13% of each run, Pallas kernels for 0% -> 0%
where the time goes in v1:
time: 327 us
  waiting for transfers between devices  198 us (61%)
  starting transfers between devices  62.4 us (19%)
  matrix products  24.9 us (8%)
  other arithmetic  15.9 us (5%)
  between operations  15.2 us (5%)
  local copies, waits for them, and re-layouts  10.5 us (3%)
    reduce_scatter x1, waiting for transfers between devices, shards(): lax.psum_scatter(terms, ('dp', 'mp'), scatter_dimension=0, tiled=True)  142 us
    ppermute x15, waiting for transfers between devices, rotated_exchange(): lax.ppermute(sent, axis, [(i, (i + step) % size) for i in range(size)])  51.3 us
    ppermute x15, starting transfers between devices, rotated_exchange(): lax.ppermute(sent, axis, [(i, (i + step) % size) for i in range(size)])  44.5 us
    dot_general x15, matrix products, contract(): lax.dot_general(left, right, (((left_dim,), (right_dim,)), ((), ())), pre...  23.6 us
    eq x1, other arithmetic, shards(): adjacency = (rowsel[:, None, :] == row_ids).astype(jnp.bfloat16)  9.71 us
    all_to_all x1, starting transfers between devices, shards(): lax.all_to_all(node_features, 'mp', split_axis=1, concat_axis=0, tiled=True)  7.39 us
  transfers between devices with their start and end apart: 19, of which 8 were waited for; matrix products, arithmetic and copies ran while one was open for 13% of the time, Pallas kernels for 0%

profile of v1, /device:TPU:0, one launch (start us, length us, event | category | flops | bytes accessed | tf_op | source)
XLA Modules:
  0.0 326.6 jit_solution(10424123492674994331)
XLA Ops:
  7.2 1.3 all_to_all.34
  9.3 7.4 %all-to-all-start = ((bf16[32,16,192]{2,0,1:T(8,128)(2,1)}), bf16[32,16,192]{2,0,1:T(8,128)(2,1)S(1)}, u32[]{:S(2)}, u32[]{:S(2)}) async-start(bf16[32,16,192]{2,0,1:T(8,128)(2,1)} %copy.42), calls=%async_computation | async-start | bytes 524288 | tf_op jit(solution)/shard_map/all_to_all | solution.py:80
  18.2 1.8 select_reduce_fusion
  20.0 9.7 %bitcast_compare_fusion = pred[3072,3072]{1,0:T(32,128)(4,1)} fusion(s32[3072]{0:T(1024)S(1)} %eq.126, s32[16,3072]{1,0:T(8,128)S(1)} %select_reduce_fusion), kind=kLoop, calls=%fused_computation | loop fusion | flops 9437184 | bytes 9646080 | tf_op jit(solution)/shard_map/layer_one_mean/eq | solution.py:71
  29.9 8.5 %fusion.1 = bf16[32,3072]{1,0:T(8,128)(2,1)S(1)} fusion(pred[3072,3072]{1,0:T(32,128)(4,1)} %bitcast_compare_fusion, bf16[32,3072]{1,0:T(8,128)(2,1)S(1)} %copy-done.6, f32[3072]{0:T(1024)S(1)} %convert_divide_fusion), kind=kOutput, calls=%fused_computation.6 | convolution fusion | flops 604176384 | bytes 9842688 | tf_op jit(solution)/shard_map/layer_one_mean/dot_general | solution.py:46
  40.4 6.1 %all-to-all-start.1 = ((bf16[32,16,192]{2,0,1:T(8,128)(2,1)}), bf16[32,16,192]{2,0,1:T(8,128)(2,1)}, u32[]{:S(2)}, u32[]{:S(2)}) async-start(bf16[32,16,192]{2,0,1:T(8,128)(2,1)} %copy.43), calls=%async_computation.1 | async-start | bytes 524288 | tf_op jit(solution)/shard_map/all_to_all | solution.py:81
  47.2 2.2 convolution_convert_fusion
  49.4 2.5 copy.46
  51.9 4.6 %all-to-all-done.1 = bf16[32,16,192]{2,0,1:T(8,128)(2,1)} async-done(((bf16[32,16,192]{2,0,1:T(8,128)(2,1)}), bf16[32,16,192]{2,0,1:T(8,128)(2,1)}, u32[]{:S(2)}, u32[]{:S(2)}) %all-to-all-start.1) | async-done | bytes 196640 | tf_op jit(solution)/shard_map/all_to_all | solution.py:81
  56.6 4.4 %all-to-all-start.2 = ((bf16[512,16,144]{0,2,1:T(8,128)(2,1)}), bf16[512,16,144]{0,2,1:T(8,128)(2,1)}, u32[]{:S(2)}, u32[]{:S(2)}) async-start(bf16[512,16,144]{0,2,1:T(8,128)(2,1)} %bitcast.33), calls=%async_computation.2 | async-start | bytes 4718592 | tf_op jit(solution)/shard_map/all_to_all | solution.py:124
  62.5 1.3 fusion.12
  64.1 1.3 fusion.21
  65.5 2.4 convolution_convert_fusion.1
  67.8 2.8 copy.45
  71.2 1.7 collective-permute-start.1
  72.9 1.4 fusion.49
  74.2 2.2 collective-permute-start.2
  76.5 1.5 collective-permute-start.3
  78.1 29.5 %collective-permute-done = bf16[1,512,144]{1,2,0:T(8,128)(2,1)S(1)} collective-permute-done((bf16[1,512,144]{1,2,0:T(8,128)(2,1)S(1)}, bf16[1,512,144]{1,2,0:T(8,128)(2,1)S(1)}, u32[]{:S(2)}, u32[]{:S(2)}) %collective-permute-start) | collective-permute-done | bytes 147488 | tf_op jit(solution)/shard_map/ppermute | solution.py:26
  108.6 16.8 %collective-permute-start.6 = (bf16[1,512,144]{1,2,0:T(8,128)(2,1)S(1)}, bf16[1,512,144]{1,2,0:T(8,128)(2,1)S(1)}, u32[]{:S(2)}, u32[]{:S(2)}) collective-permute-start(bf16[1,512,144]{1,2,0:T(8,128)(2,1)S(1)} %get-tuple-element.10), channel_id=1, source_target_pairs={{0,7},{1,8},{2,9},{3,10},{4,11},{5,12},{6,13},{7,14},{8,15},{9,0},... | collective-permute-start | bytes 442376 | tf_op jit(solution)/shard_map/ppermute | solution.py:26
  125.5 2.5 collective-permute-start.8
  128.1 16.5 %collective-permute-done.4 = bf16[1,512,144]{1,2,0:T(8,128)(2,1)S(1)} collective-permute-done((bf16[1,512,144]{1,2,0:T(8,128)(2,1)S(1)}, bf16[1,512,144]{1,2,0:T(8,128)(2,1)S(1)}, u32[]{:S(2)}, u32[]{:S(2)}) %collective-permute-start.4) | collective-permute-done | bytes 147488 | tf_op jit(solution)/shard_map/ppermute | solution.py:26
  145.5 1.5 collective-permute-start.10
  147.0 7.7 %collective-permute-start.11 = (bf16[1,512,144]{1,2,0:T(8,128)(2,1)S(1)}, bf16[1,512,144]{1,2,0:T(8,128)(2,1)S(1)}, u32[]{:S(2)}, u32[]{:S(2)}) collective-permute-start(bf16[1,512,144]{1,2,0:T(8,128)(2,1)S(1)} %get-tuple-element.5), channel_id=1, source_target_pairs={{0,12},{1,13},{2,14},{3,15},{4,0},{5,1},{6,2},{7,3},{8,4},{9,5},{1... | collective-permute-start | bytes 442376 | tf_op jit(solution)/shard_map/ppermute | solution.py:26
  154.7 1.1 collective-permute-start.12
  155.8 5.3 %collective-permute-start.13 = (bf16[1,512,144]{1,2,0:T(8,128)(2,1)S(1)}, bf16[1,512,144]{1,2,0:T(8,128)(2,1)S(1)}, u32[]{:S(2)}, u32[]{:S(2)}) collective-permute-start(bf16[1,512,144]{1,2,0:T(8,128)(2,1)S(1)} %get-tuple-element.3), channel_id=1, source_target_pairs={{0,14},{1,15},{2,0},{3,1},{4,2},{5,3},{6,4},{7,5},{8,6},{9,7},{10,... | collective-permute-start | bytes 442376 | tf_op jit(solution)/shard_map/ppermute | solution.py:26
  161.1 3.7 %collective-permute-start.14 = (bf16[1,512,144]{1,2,0:T(8,128)(2,1)S(1)}, bf16[1,512,144]{1,2,0:T(8,128)(2,1)S(1)}, u32[]{:S(2)}, u32[]{:S(2)}) collective-permute-start(bf16[1,512,144]{1,2,0:T(8,128)(2,1)S(1)} %get-tuple-element.2), channel_id=1, source_target_pairs={{0,15},{1,0},{2,1},{3,2},{4,3},{5,4},{6,5},{7,6},{8,7},{9,8},{10,9... | collective-permute-start | bytes 442376 | tf_op jit(solution)/shard_map/ppermute | solution.py:26
  164.9 3.1 collective-permute-done.13
  169.6 2.7 convolution_bitcast_fusion.1
  172.8 1.2 fusion.50
  174.3 2.4 pad_maximum_fusion
  178.0 141.8 %reduce-scatter.2.cloned.1.call-done = f32[64,512]{1,0:T(8,128)} async-done(((f32[2048,512]{1,0:T(8,128)}), f32[64,512]{1,0:T(8,128)}) %reduce-scatter.2.cloned.1.call-update) | async-done | bytes 131088 | tf_op jit(solution)/shard_map/reduce_scatter | solution.py:137
  (83 shorter events, 12.5 us)
Async XLA Ops:
  7.2 40.0 %copy-start = (bf16[192,512]{1,0:T(8,128)(2,1)S(1)}, bf16[192,512]{1,0:T(8,128)(2,1)}, u32[]{:S(2)}) copy-start(bf16[192,512]{1,0:T(8,128)(2,1)} %param.13) | copy-start | bytes 589828
  9.3 31.1 %all-to-all-start = ((bf16[32,16,192]{2,0,1:T(8,128)(2,1)}), bf16[32,16,192]{2,0,1:T(8,128)(2,1)S(1)}, u32[]{:S(2)}, u32[]{:S(2)}) async-start(bf16[32,16,192]{2,0,1:T(8,128)(2,1)} %copy.42), calls=%async_computation | async-start | bytes 524288 | tf_op jit(solution)/shard_map/all_to_all | solution.py:80
  20.0 9.9 %copy-start.6 = (bf16[32,3072]{1,0:T(8,128)(2,1)S(1)}, bf16[32,3072]{1,0:T(8,128)(2,1)}, u32[]{:S(2)}) copy-start(bf16[32,3072]{1,0:T(8,128)(2,1)} %param.7) | copy-start | bytes 589828
  39.0 7.7 %copy-start.1 = (s32[16,16,192]{2,1,0:T(8,128)}, s32[16,16,192]{2,1,0:T(8,128)S(1)}, u32[]{:S(2)}) copy-start(s32[16,16,192]{2,1,0:T(8,128)S(1)} %reduce_max.12) | copy-start | bytes 589828
  40.3 6.4 %copy-start.5 = (s32[256,192]{1,0:T(8,128)}, s32[256,192]{1,0:T(8,128)S(1)}, u32[]{:S(2)}) copy-start(s32[256,192]{1,0:T(8,128)S(1)} %copy.44) | copy-start | bytes 589828
  40.4 16.2 %all-to-all-start.1 = ((bf16[32,16,192]{2,0,1:T(8,128)(2,1)}), bf16[32,16,192]{2,0,1:T(8,128)(2,1)}, u32[]{:S(2)}, u32[]{:S(2)}) async-start(bf16[32,16,192]{2,0,1:T(8,128)(2,1)} %copy.43), calls=%async_computation.1 | async-start | bytes 524288 | tf_op jit(solution)/shard_map/all_to_all | solution.py:81
  56.6 113.1 %all-to-all-start.2 = ((bf16[512,16,144]{0,2,1:T(8,128)(2,1)}), bf16[512,16,144]{0,2,1:T(8,128)(2,1)}, u32[]{:S(2)}, u32[]{:S(2)}) async-start(bf16[512,16,144]{0,2,1:T(8,128)(2,1)} %bitcast.33), calls=%async_computation.2 | async-start | bytes 4718592 | tf_op jit(solution)/shard_map/all_to_all | solution.py:124
  61.0 2.8 copy-start.2
  61.0 258.7 %reduce-scatter.2.cloned.1.call-start = ((), (), s32[]{:S(2)}) async-start(), calls=%async_computation.4 | async-start | bytes 4325376 | tf_op jit(solution)/shard_map/reduce_scatter | solution.py:137
  63.8 1.7 copy-start.7
  70.9 36.8 %collective-permute-start = (bf16[1,512,144]{1,2,0:T(8,128)(2,1)S(1)}, bf16[1,512,144]{1,2,0:T(8,128)(2,1)S(1)}, u32[]{:S(2)}, u32[]{:S(2)}) collective-permute-start(bf16[1,512,144]{1,2,0:T(8,128)(2,1)S(1)} %get-tuple-element.16), channel_id=1, source_target_pairs={{0,1},{1,2},{2,3},{3,4},{4,5},{5,6},{6,7},{7,8},{8,9},{9,10},{10,1... | collective-permute-start | bytes 442376 | tf_op jit(solution)/shard_map/ppermute | solution.py:26
  71.2 37.4 %collective-permute-start.1 = (bf16[1,512,144]{1,2,0:T(8,128)(2,1)S(1)}, bf16[1,512,144]{1,2,0:T(8,128)(2,1)S(1)}, u32[]{:S(2)}, u32[]{:S(2)}) collective-permute-start(bf16[1,512,144]{1,2,0:T(8,128)(2,1)S(1)} %get-tuple-element.15), channel_id=1, source_target_pairs={{0,2},{1,3},{2,4},{3,5},{4,6},{5,7},{6,8},{7,9},{8,10},{9,11},{10,... | collective-permute-start | bytes 442376 | tf_op jit(solution)/shard_map/ppermute | solution.py:26
  74.2 51.2 %collective-permute-start.2 = (bf16[1,512,144]{1,2,0:T(8,128)(2,1)S(1)}, bf16[1,512,144]{1,2,0:T(8,128)(2,1)S(1)}, u32[]{:S(2)}, u32[]{:S(2)}) collective-permute-start(bf16[1,512,144]{1,2,0:T(8,128)(2,1)S(1)} %get-tuple-element.14), channel_id=1, source_target_pairs={{0,3},{1,4},{2,5},{3,6},{4,7},{5,8},{6,9},{7,10},{8,11},{9,12},{10... | collective-permute-start | bytes 442376 | tf_op jit(solution)/shard_map/ppermute | solution.py:26
  76.5 49.0 %collective-permute-start.3 = (bf16[1,512,144]{1,2,0:T(8,128)(2,1)S(1)}, bf16[1,512,144]{1,2,0:T(8,128)(2,1)S(1)}, u32[]{:S(2)}, u32[]{:S(2)}) collective-permute-start(bf16[1,512,144]{1,2,0:T(8,128)(2,1)S(1)} %get-tuple-element.13), channel_id=1, source_target_pairs={{0,4},{1,5},{2,6},{3,7},{4,8},{5,9},{6,10},{7,11},{8,12},{9,13},{1... | collective-permute-start | bytes 442376 | tf_op jit(solution)/shard_map/ppermute | solution.py:26
  78.0 66.6 %collective-permute-start.4 = (bf16[1,512,144]{1,2,0:T(8,128)(2,1)S(1)}, bf16[1,512,144]{1,2,0:T(8,128)(2,1)S(1)}, u32[]{:S(2)}, u32[]{:S(2)}) collective-permute-start(bf16[1,512,144]{1,2,0:T(8,128)(2,1)S(1)} %get-tuple-element.12), channel_id=1, source_target_pairs={{0,5},{1,6},{2,7},{3,8},{4,9},{5,10},{6,11},{7,12},{8,13},{9,14},{... | collective-permute-start | bytes 442376 | tf_op jit(solution)/shard_map/ppermute | solution.py:26
  107.7 37.8 %collective-permute-start.5 = (bf16[1,512,144]{1,2,0:T(8,128)(2,1)S(1)}, bf16[1,512,144]{1,2,0:T(8,128)(2,1)S(1)}, u32[]{:S(2)}, u32[]{:S(2)}) collective-permute-start(bf16[1,512,144]{1,2,0:T(8,128)(2,1)S(1)} %get-tuple-element.11), channel_id=1, source_target_pairs={{0,6},{1,7},{2,8},{3,9},{4,10},{5,11},{6,12},{7,13},{8,14},{9,15},... | collective-permute-start | bytes 442376 | tf_op jit(solution)/shard_map/ppermute | solution.py:26
  108.6 38.4 %collective-permute-start.6 = (bf16[1,512,144]{1,2,0:T(8,128)(2,1)S(1)}, bf16[1,512,144]{1,2,0:T(8,128)(2,1)S(1)}, u32[]{:S(2)}, u32[]{:S(2)}) collective-permute-start(bf16[1,512,144]{1,2,0:T(8,128)(2,1)S(1)} %get-tuple-element.10), channel_id=1, source_target_pairs={{0,7},{1,8},{2,9},{3,10},{4,11},{5,12},{6,13},{7,14},{8,15},{9,0},... | collective-permute-start | bytes 442376 | tf_op jit(solution)/shard_map/ppermute | solution.py:26
  125.4 29.3 %collective-permute-start.7 = (bf16[1,512,144]{1,2,0:T(8,128)(2,1)S(1)}, bf16[1,512,144]{1,2,0:T(8,128)(2,1)S(1)}, u32[]{:S(2)}, u32[]{:S(2)}) collective-permute-start(bf16[1,512,144]{1,2,0:T(8,128)(2,1)S(1)} %get-tuple-element.9), channel_id=1, source_target_pairs={{0,8},{1,9},{2,10},{3,11},{4,12},{5,13},{6,14},{7,15},{8,0},{9,1},... | collective-permute-start | bytes 442376 | tf_op jit(solution)/shard_map/ppermute | solution.py:26
  125.5 30.3 %collective-permute-start.8 = (bf16[1,512,144]{1,2,0:T(8,128)(2,1)S(1)}, bf16[1,512,144]{1,2,0:T(8,128)(2,1)S(1)}, u32[]{:S(2)}, u32[]{:S(2)}) collective-permute-start(bf16[1,512,144]{1,2,0:T(8,128)(2,1)S(1)} %get-tuple-element.8), channel_id=1, source_target_pairs={{0,9},{1,10},{2,11},{3,12},{4,13},{5,14},{6,15},{7,0},{8,1},{9,2},... | collective-permute-start | bytes 442376 | tf_op jit(solution)/shard_map/ppermute | solution.py:26
  144.5 16.6 %collective-permute-start.9 = (bf16[1,512,144]{1,2,0:T(8,128)(2,1)S(1)}, bf16[1,512,144]{1,2,0:T(8,128)(2,1)S(1)}, u32[]{:S(2)}, u32[]{:S(2)}) collective-permute-start(bf16[1,512,144]{1,2,0:T(8,128)(2,1)S(1)} %get-tuple-element.7), channel_id=1, source_target_pairs={{0,10},{1,11},{2,12},{3,13},{4,14},{5,15},{6,0},{7,1},{8,2},{9,3},... | collective-permute-start | bytes 442376 | tf_op jit(solution)/shard_map/ppermute | solution.py:26
  145.5 19.4 %collective-permute-start.10 = (bf16[1,512,144]{1,2,0:T(8,128)(2,1)S(1)}, bf16[1,512,144]{1,2,0:T(8,128)(2,1)S(1)}, u32[]{:S(2)}, u32[]{:S(2)}) collective-permute-start(bf16[1,512,144]{1,2,0:T(8,128)(2,1)S(1)} %get-tuple-element.6), channel_id=1, source_target_pairs={{0,11},{1,12},{2,13},{3,14},{4,15},{5,0},{6,1},{7,2},{8,3},{9,4},{... | collective-permute-start | bytes 442376 | tf_op jit(solution)/shard_map/ppermute | solution.py:26
  147.0 17.9 %collective-permute-start.11 = (bf16[1,512,144]{1,2,0:T(8,128)(2,1)S(1)}, bf16[1,512,144]{1,2,0:T(8,128)(2,1)S(1)}, u32[]{:S(2)}, u32[]{:S(2)}) collective-permute-start(bf16[1,512,144]{1,2,0:T(8,128)(2,1)S(1)} %get-tuple-element.5), channel_id=1, source_target_pairs={{0,12},{1,13},{2,14},{3,15},{4,0},{5,1},{6,2},{7,3},{8,4},{9,5},{1... | collective-permute-start | bytes 442376 | tf_op jit(solution)/shard_map/ppermute | solution.py:26
  154.7 10.2 %collective-permute-start.12 = (bf16[1,512,144]{1,2,0:T(8,128)(2,1)S(1)}, bf16[1,512,144]{1,2,0:T(8,128)(2,1)S(1)}, u32[]{:S(2)}, u32[]{:S(2)}) collective-permute-start(bf16[1,512,144]{1,2,0:T(8,128)(2,1)S(1)} %get-tuple-element.4), channel_id=1, source_target_pairs={{0,13},{1,14},{2,15},{3,0},{4,1},{5,2},{6,3},{7,4},{8,5},{9,6},{10... | collective-permute-start | bytes 442376 | tf_op jit(solution)/shard_map/ppermute | solution.py:26
  155.8 12.2 %collective-permute-start.13 = (bf16[1,512,144]{1,2,0:T(8,128)(2,1)S(1)}, bf16[1,512,144]{1,2,0:T(8,128)(2,1)S(1)}, u32[]{:S(2)}, u32[]{:S(2)}) collective-permute-start(bf16[1,512,144]{1,2,0:T(8,128)(2,1)S(1)} %get-tuple-element.3), channel_id=1, source_target_pairs={{0,14},{1,15},{2,0},{3,1},{4,2},{5,3},{6,4},{7,5},{8,6},{9,7},{10,... | collective-permute-start | bytes 442376 | tf_op jit(solution)/shard_map/ppermute | solution.py:26
  161.1 7.2 %collective-permute-start.14 = (bf16[1,512,144]{1,2,0:T(8,128)(2,1)S(1)}, bf16[1,512,144]{1,2,0:T(8,128)(2,1)S(1)}, u32[]{:S(2)}, u32[]{:S(2)}) collective-permute-start(bf16[1,512,144]{1,2,0:T(8,128)(2,1)S(1)} %get-tuple-element.2), channel_id=1, source_target_pairs={{0,15},{1,0},{2,1},{3,2},{4,3},{5,4},{6,5},{7,6},{8,7},{9,8},{10,9... | collective-permute-start | bytes 442376 | tf_op jit(solution)/shard_map/ppermute | solution.py:26
  169.6 2.8 copy-start.3
  172.4 1.9 copy-start.4
Sparse Core Ops, SparseCore 0:
  176.8 142.8 reduce-scatter.1
